TPU v7x, 256 devices: a whole 4x4x8 slice. The times are simulated.
256 devices in a mesh: section: 2 (over core), tok: 32 (over z, y), rep: 4 (over x).
Axes of the slice: x: 4, y: 4, z: 8, core: 2. Of those that a mesh axis runs over, the one named last changes fastest.
Arguments:
- inputs: bfloat16 [2, 4096, 1024], P(None, 'tok')
- segment_ids: int32 [2, 4096], replicated, may hold values from 0 to 7, as said below
- picks: int32 [2, 4096, 2], P(None, 'tok'), may hold values from 0 to 15, all different within a row; in each aligned block of 128 rows (0 to 127, 128 to 255, ..., all dimensions but the last counted through in order) at most 20 rows name the same one
- page_table: int32 [2, 32], replicated, may hold values from 0 to 31, each once within a row
- norm_gains: float32 [2, 2, 1024], P('section'), may hold values from 0.1 to 1.9
- attn_qkv: bfloat16 [2, 1024, 3, 1024], P('section', None, None, 'rep')
- attn_out: bfloat16 [2, 1024, 1024], P('section', 'rep'), may hold values from -0.1875 to 0.1875
- router: bfloat16 [2, 1024, 16], P('section')
- expert_in: bfloat16 [2, 32, 1024, 2, 1408], P('section', 'tok', None, None, 'rep'), may hold values from -0.1875 to 0.1875
- expert_out: bfloat16 [2, 32, 1408, 1024], P('section', 'tok', 'rep')
Outputs:
- layer_out: bfloat16 [2, 2, 4096, 1024], P('section', None, 'tok')
- kv_pages: bfloat16 [2, 2, 32, 128, 2, 1024], P('section', None, 'tok', None, None, 'rep')
Inputs may be any that keep to these rules, and one draw needn't show every extreme that they name: `picks`: within the tokens of one index of tok in one micro-batch, at most 20 tokens pick one expert, and some expert is picked by exactly 20. `segment_ids`: ids never fall along a micro-batch; every prompt has at least one token, a prompt spans at most 2048 tokens and one spans exactly 2048. `page_table`: each row is a permutation.
All inputs are finite; a program needn't handle non-finite values.
Results may differ from a plain program's by a relative error of at most 0.034.
Values may be sent and summed in bfloat16 or wider, within the bound.
No kernel may reach another device: no remote copies, remote signals or barrier semaphores. Data moves between devices by JAX's collectives and lax.ppermute only.
A program may use at most 128 MiB of HBM per device.

v0:
```python
import jax
import jax.numpy as jnp
from jax import lax
from jax.sharding import PartitionSpec as P

HEAD_DIM = 64
TOP = 2
PAGE = 128
CAP = 20
NEG_FILL = -1e30


def shifted(value, axis, steps):
    count = lax.axis_size(axis)
    first, last = (max(0, -steps), min(count, count - steps))
    return lax.ppermute(value, axis, [(source, source + steps) for source in range(first, last)])


def rms_scale(values, gains):
    return values * lax.rsqrt(jnp.mean(values * values, axis=-1, keepdims=True) + 1e-06) * gains


def attend(carry, queries, keys_vals, seg_query, pos_query, seg_key, pos_key):
    run_max, run_sum, run_acc = carry
    heads_here = run_acc.shape[0]
    head_size = run_acc.shape[2]
    rows_key = keys_vals.shape[0]
    key_part = keys_vals[:, 0].reshape(rows_key, heads_here, head_size)
    val_part = keys_vals[:, 1].reshape(rows_key, heads_here, head_size).astype(jnp.float32)
    scores = jnp.einsum(
        "thd,nhd->htn", queries, key_part, preferred_element_type=jnp.float32
    ) * head_size ** (-0.5)
    visible = (seg_query[:, None] == seg_key[None, :]) & (pos_query[:, None] >= pos_key[None, :])
    masked = jnp.where(visible[None], scores, NEG_FILL)
    new_max = jnp.maximum(run_max, jnp.max(masked, axis=-1))
    weights = jnp.where(visible[None], jnp.exp(masked - new_max[..., None]), 0.0)
    decay = jnp.exp(run_max - new_max)
    run_sum = run_sum * decay + jnp.sum(weights, axis=-1)
    run_acc = run_acc * decay[..., None] + jnp.einsum(
        "htn,nhd->htd", weights, val_part, precision=lax.Precision.HIGHEST
    )
    return (new_max, run_sum, run_acc)


def place_pages(pages, keys_vals, table_row, tok_index):
    rows_here = keys_vals.shape[0]
    blocks_dev = pages.shape[0]
    page_rows = pages.shape[1]
    block_ids = jnp.arange(table_row.shape[0], dtype=jnp.int32)
    wanted = tok_index * blocks_dev + 0
    source = jnp.sum(jnp.where(table_row == wanted, block_ids, 0))
    offset = source * page_rows
    inside = (offset >= 0) & (offset + page_rows <= rows_here)
    block = lax.dynamic_slice_in_dim(
        keys_vals, jnp.clip(offset, 0, rows_here - page_rows), page_rows, 0
    )
    updated = [jnp.where(inside, block, pages[0])]
    return jnp.stack(updated)


def per_device(
    inputs,
    segment_ids,
    picks,
    page_table,
    norm_gains,
    attn_qkv,
    attn_out,
    router,
    expert_in,
    expert_out,
):
    section_index = lax.axis_index("section")
    tok_index = lax.axis_index("tok")
    tok_count = lax.axis_size("tok")
    micro_count = inputs.shape[0]
    tok_rows = inputs.shape[1]
    width = inputs.shape[2]
    col_width = attn_qkv.shape[3]
    head_count = col_width // HEAD_DIM
    experts_all = router.shape[2]
    local_pieces = expert_in.shape[1]
    split_count = local_pieces * tok_count // experts_all
    blocks_dev = tok_rows // PAGE
    row_ids = jnp.arange(tok_rows, dtype=jnp.int32)
    pos_query = tok_index * tok_rows + row_ids
    gains = norm_gains[0]
    w_qkv = attn_qkv[0].reshape(width, 3 * col_width)
    w_out = attn_out[0]
    w_router = router[0]
    w_in = expert_in[0]
    w_down = expert_out[0]
    outputs = [jnp.zeros((tok_rows, width), jnp.bfloat16) for slot_micro in range(micro_count)]
    page_out = [
        jnp.zeros((blocks_dev, PAGE, 2, col_width), jnp.bfloat16)
        for slot_micro in range(micro_count)
    ]
    received = jnp.zeros((tok_rows, width), jnp.bfloat16)
    for round_index in range(micro_count + 1):
        own_micro = round_index - section_index
        micro_index = jnp.clip(own_micro, 0, micro_count - 1)
        fresh = inputs[min(round_index, micro_count - 1)]
        layer_in = jnp.where(section_index == 0, fresh, received)
        seg_all = lax.dynamic_index_in_dim(segment_ids, micro_index, 0, keepdims=False)
        seg_query = lax.dynamic_slice_in_dim(seg_all, tok_index * tok_rows, tok_rows)
        table_row = lax.dynamic_index_in_dim(page_table, micro_index, 0, keepdims=False)
        pick_rows = lax.dynamic_index_in_dim(picks, micro_index, 0, keepdims=False)
        resid = layer_in.astype(jnp.float32)
        normed = rms_scale(resid, gains[0]).astype(jnp.bfloat16)
        projected = jnp.dot(normed, w_qkv, preferred_element_type=jnp.float32).astype(jnp.bfloat16)
        projected = projected.reshape(tok_rows, 3, col_width)
        queries = projected[:, 0].reshape(tok_rows, head_count, HEAD_DIM)
        keys_vals = projected[:, 1:]
        soft_init = (
            jnp.full((head_count, tok_rows), NEG_FILL, jnp.float32),
            jnp.zeros((head_count, tok_rows), jnp.float32),
            jnp.zeros((head_count, tok_rows, HEAD_DIM), jnp.float32),
        )
        empty_pages = jnp.zeros((blocks_dev, PAGE, 2, col_width), jnp.bfloat16)
        piece = lax.all_gather(keys_vals, "tok", axis=0, tiled=True)
        rows_key = piece.shape[0]
        step_rows = 1024
        while rows_key % step_rows != 0:
            step_rows = step_rows // 2
        turns = rows_key // step_rows

        def key_block(index, soft_now):
            start = index * step_rows
            block = lax.dynamic_slice_in_dim(piece, start, step_rows, 0)
            seg_key = lax.dynamic_slice_in_dim(seg_all, start, step_rows)
            pos_key = start + jnp.arange(step_rows, dtype=jnp.int32)
            return attend(soft_now, queries, block, seg_query, pos_query, seg_key, pos_key)

        soft_next = lax.fori_loop(0, turns, key_block, soft_init)
        pages = place_pages(empty_pages, piece, table_row, tok_index)
        run_max, run_sum, run_acc = soft_next
        context = (
            (run_acc / run_sum[..., None])
            .transpose(1, 0, 2)
            .reshape(tok_rows, col_width)
            .astype(jnp.bfloat16)
        )
        attn_part = jnp.dot(context, w_out, preferred_element_type=jnp.float32)
        mid = resid + lax.psum(attn_part, "rep")
        normed_mid = rms_scale(mid, gains[1]).astype(jnp.bfloat16)
        logits = jnp.dot(normed_mid, w_router, preferred_element_type=jnp.float32)
        expert_ids = jnp.arange(experts_all, dtype=jnp.int32)
        chosen = (pick_rows[:, :, None] == expert_ids[None, None, :]).astype(jnp.int32)
        picked_logit = jnp.sum(chosen.astype(jnp.float32) * logits[:, None, :], axis=-1)
        top_logit = jnp.max(picked_logit, axis=-1, keepdims=True)
        raised = jnp.exp(picked_logit - top_logit)
        gate_vals = raised / jnp.sum(raised, axis=-1, keepdims=True)
        ordered = chosen.transpose(1, 0, 2).reshape(TOP * tok_rows, experts_all)
        slot_of = jnp.sum((jnp.cumsum(ordered, axis=0) - 1) * ordered, axis=-1)
        flat_slot = pick_rows.T.reshape(TOP * tok_rows) * CAP + slot_of
        slot_ids = jnp.arange(experts_all * CAP, dtype=jnp.int32)
        hits = (flat_slot[:, None] == slot_ids[None, :]).astype(jnp.int32)
        hits = jnp.sum(hits.reshape(TOP, tok_rows, experts_all * CAP), axis=0).astype(jnp.bfloat16)
        dispatch = lax.dot_general(
            hits, normed_mid, (((0,), (0,)), ((), ())), preferred_element_type=jnp.float32
        ).astype(jnp.bfloat16)
        copies = jnp.broadcast_to(
            dispatch.reshape(experts_all, 1, CAP, width), (experts_all, split_count, CAP, width)
        )
        copies = copies.reshape(tok_count, local_pieces, CAP, width)
        act = jnp.einsum(
            "secd,edgf->secgf",
            lax.all_to_all(copies, "tok", split_axis=0, concat_axis=0, tiled=True),
            w_in,
            preferred_element_type=jnp.float32,
        )
        hidden = (jax.nn.gelu(act[..., 0, :]) * act[..., 1, :]).astype(jnp.bfloat16)
        returned = lax.all_to_all(
            jnp.einsum("secf,efd->secd", hidden, w_down, preferred_element_type=jnp.float32).astype(
                jnp.bfloat16
            ),
            "tok",
            split_axis=0,
            concat_axis=0,
            tiled=True,
        )
        summed = jnp.sum(
            returned.reshape(experts_all, split_count, CAP, width).astype(jnp.float32), axis=1
        )
        summed = summed.reshape(experts_all * CAP, width)
        gathered = jnp.take(summed, flat_slot, axis=0).reshape(TOP, tok_rows, width)
        expert_local = jnp.sum(gate_vals.T[:, :, None] * gathered, axis=0)
        expert_total = lax.psum(expert_local, "rep")
        layer_result = (mid + expert_total).astype(jnp.bfloat16)
        for slot_micro in range(micro_count):
            if slot_micro == round_index or slot_micro == round_index - 1:
                taken = own_micro == slot_micro
                outputs[slot_micro] = jnp.where(taken, layer_result, outputs[slot_micro])
                page_out[slot_micro] = jnp.where(taken, pages, page_out[slot_micro])
        if round_index < micro_count:
            received = shifted(layer_result, "section", 1)
    return (jnp.stack(outputs)[None], jnp.stack(page_out)[None])


def solution(mesh):
    return jax.shard_map(
        per_device,
        mesh=mesh,
        in_specs=(
            P(None, "tok", None),
            P(),
            P(None, "tok", None),
            P(),
            P("section", None, None),
            P("section", None, None, "rep"),
            P("section", "rep", None),
            P("section", None, None),
            P("section", "tok", None, None, "rep"),
            P("section", "tok", "rep", None),
        ),
        out_specs=(P("section", None, "tok", None), P("section", None, "tok", None, None, "rep")),
        check_vma=False,
    )
```

profile of v0, /device:TPU:8, one launch (start us, length us, event | category | flops | bytes accessed | tf_op | source)
XLA Modules:
  0.0 1003.8 jit_solution(15672951469307340651)
XLA Ops:
  9.3 1.7 copy.83
  20.4 79.9 %all-gather.4.cloned.1.call-done = bf16[4096,2,256]{0,2,1:T(8,128)(2,1)} async-done(((bf16[128,2,256]{0,2,1:T(8,128)(2,1)}), bf16[4096,2,256]{0,2,1:T(8,128)(2,1)}) %all-gather.4.cloned.1.call-update) | async-done | bytes 4194320 | tf_op jit(solution)/shard_map/all_gather | solution.py:120
  100.3 34.9 %while.54 = (s32[]{:T(128)}, f32[4,128]{1,0:T(4,128)S(1)}, f32[4,128]{1,0:T(4,128)S(1)}, f32[4,128,64]{1,2,0:T(8,128)}, s32[128]{0:T(128)}, /*index=5*/s32[4096]...) while((s32[]{:T(128)}, f32[4,128]{1,0:T(4,128)S(1)}, ...), condition=%wide.region_4.5_spmd.clone, body=%wide.region_1.4_spmd.clone.sunk | while | flops 476548736 | bytes 14800775 | solution.py:134
  102.7 2.1 constant_dynamic-slice_fusion.18
  111.4 2.1 constant_dynamic-slice_fusion.18
  120.1 2.1 constant_dynamic-slice_fusion.18
  128.9 2.1 constant_dynamic-slice_fusion.18
  136.2 2.1 fusion.102
  140.8 46.1 %all-reduce.7.cloned.1.call-done = f32[128,1024]{1,0:T(8,128)} async-done(((f32[128,1024]{1,0:T(8,128)}), f32[128,1024]{1,0:T(8,128)}) %all-reduce.7.cloned.1.call-update) | async-done | bytes 524304 | tf_op jit(solution)/shard_map/psum | solution.py:144
  190.6 47.1 %all_to_all.30 = bf16[32,1,20,1024]{3,2,1,0:T(8,128)(2,1)S(1)} all-to-all(bf16[32,1,20,1024]{3,2,1,0:T(8,128)(2,1)S(1)} %bitcast.386), channel_id=1, replica_groups=mesh['section'=2,'tok'=32,'rep'=4] {'tok'}, dimensions={0} | all-to-all | bytes 2621440 | tf_op jit(solution)/shard_map/all_to_all | solution.py:168
  237.7 1.8 convolution_bitcast_fusion.2
  240.4 1.9 copy.87
  242.3 5.7 all-to-all-start.1
  251.2 33.0 %all-to-all-done.1 = bf16[32,1,20,1024]{3,2,1,0:T(8,128)(2,1)S(1)} async-done(((bf16[32,1,20,1024]{3,2,1,0:T(8,128)(2,1)}), bf16[32,1,20,1024]{3,2,1,0:T(8,128)(2,1)S(1)}, u32[]{:S(2)}, u32[]{:S(2)}) %all-to-all-start.1) | async-done | bytes 1310752 | tf_op jit(solution)/shard_map/all_to_all | solution.py:173
  287.2 2.2 gather_fusion
  291.7 45.9 %all-reduce.9.cloned.1.call-done = f32[128,1024]{1,0:T(8,128)} async-done(((f32[128,1024]{1,0:T(8,128)}), f32[128,1024]{1,0:T(8,128)}) %all-reduce.9.cloned.1.call-update) | async-done | bytes 524304 | tf_op jit(solution)/shard_map/psum | solution.py:188
  348.5 79.2 %all-gather.6.cloned.1.call-done = bf16[4096,2,256]{0,2,1:T(8,128)(2,1)} async-done(((bf16[128,2,256]{0,2,1:T(8,128)(2,1)}), bf16[4096,2,256]{0,2,1:T(8,128)(2,1)}) %all-gather.6.cloned.1.call-update) | async-done | bytes 4194320 | tf_op jit(solution)/shard_map/all_gather | solution.py:120
  427.7 35.0 %while.55 = (s32[]{:T(128)}, f32[4,128]{1,0:T(4,128)S(1)}, f32[4,128]{1,0:T(4,128)S(1)}, f32[4,128,64]{1,2,0:T(8,128)}, s32[128]{0:T(128)}, /*index=5*/s32[4096]...) while((s32[]{:T(128)}, f32[4,128]{1,0:T(4,128)S(1)}, ...), condition=%wide.region_21.23_spmd.clone, body=%wide.region_18.22_spmd.clone.sunk | while | flops 476548736 | bytes 14800775 | solution.py:134
  430.1 2.1 constant_dynamic-slice_fusion.19
  438.8 2.1 constant_dynamic-slice_fusion.19
  447.5 2.1 constant_dynamic-slice_fusion.19
  456.3 2.1 constant_dynamic-slice_fusion.19
  463.6 2.1 fusion.100
  468.8 45.5 %all-reduce.11.cloned.1.call-done = f32[128,1024]{1,0:T(8,128)} async-done(((f32[128,1024]{1,0:T(8,128)}), f32[128,1024]{1,0:T(8,128)}) %all-reduce.11.cloned.1.call-update) | async-done | bytes 524304 | tf_op jit(solution)/shard_map/psum | solution.py:144
  517.3 47.1 %all_to_all.31 = bf16[32,1,20,1024]{3,2,1,0:T(8,128)(2,1)S(1)} all-to-all(bf16[32,1,20,1024]{3,2,1,0:T(8,128)(2,1)S(1)} %bitcast.387), channel_id=1, replica_groups=mesh['section'=2,'tok'=32,'rep'=4] {'tok'}, dimensions={0} | all-to-all | bytes 2621440 | tf_op jit(solution)/shard_map/all_to_all | solution.py:168
  564.4 1.8 convolution_bitcast_fusion.1
  567.1 1.9 copy.93
  569.0 5.7 all-to-all-start.3
  577.6 33.2 %all-to-all-done.3 = bf16[32,1,20,1024]{3,2,1,0:T(8,128)(2,1)S(1)} async-done(((bf16[32,1,20,1024]{3,2,1,0:T(8,128)(2,1)}), bf16[32,1,20,1024]{3,2,1,0:T(8,128)(2,1)S(1)}, u32[]{:S(2)}, u32[]{:S(2)}) %all-to-all-start.3) | async-done | bytes 1310752 | tf_op jit(solution)/shard_map/all_to_all | solution.py:173
  613.8 2.2 gather_fusion.1
  618.5 46.1 %all-reduce.13.cloned.1.call-done = f32[128,1024]{1,0:T(8,128)} async-done(((f32[128,1024]{1,0:T(8,128)}), f32[128,1024]{1,0:T(8,128)}) %all-reduce.13.cloned.1.call-update) | async-done | bytes 524304 | tf_op jit(solution)/shard_map/psum | solution.py:188
  664.5 2.1 select_bitcast_fusion
  672.4 82.9 %all-gather.8.cloned.1.call-done = bf16[4096,2,256]{0,2,1:T(8,128)(2,1)} async-done(((bf16[128,2,256]{0,2,1:T(8,128)(2,1)}), bf16[4096,2,256]{0,2,1:T(8,128)(2,1)}) %all-gather.8.cloned.1.call-update) | async-done | bytes 4194320 | tf_op jit(solution)/shard_map/all_gather | solution.py:120
  755.3 34.7 %while.56 = (s32[]{:T(128)}, f32[4,128]{1,0:T(4,128)S(1)}, f32[4,128]{1,0:T(4,128)S(1)}, f32[4,128,64]{1,2,0:T(8,128)}, s32[128]{0:T(128)}, /*index=5*/s32[4096]...) while((s32[]{:T(128)}, f32[4,128]{1,0:T(4,128)S(1)}, ...), condition=%wide.region_38.40_spmd.clone, body=%wide.region_35.39_spmd.clone.sunk | while | flops 476548736 | bytes 14800775 | solution.py:134
  757.6 2.1 constant_dynamic-slice_fusion.20
  766.3 2.1 constant_dynamic-slice_fusion.20
  775.0 2.1 constant_dynamic-slice_fusion.20
  783.7 2.1 constant_dynamic-slice_fusion.20
  791.0 2.1 fusion.98
  793.9 47.8 %all-reduce.15.cloned.1.call-done = f32[128,1024]{1,0:T(8,128)} async-done(((f32[128,1024]{1,0:T(8,128)}), f32[128,1024]{1,0:T(8,128)}) %all-reduce.15.cloned.1.call-update) | async-done | bytes 524304 | tf_op jit(solution)/shard_map/psum | solution.py:144
  846.6 47.1 %all_to_all.32 = bf16[32,1,20,1024]{3,2,1,0:T(8,128)(2,1)S(1)} all-to-all(bf16[32,1,20,1024]{3,2,1,0:T(8,128)(2,1)S(1)} %bitcast.388), channel_id=1, replica_groups=mesh['section'=2,'tok'=32,'rep'=4] {'tok'}, dimensions={0} | all-to-all | bytes 2621440 | tf_op jit(solution)/shard_map/all_to_all | solution.py:168
  893.7 1.8 convolution_bitcast_fusion
  896.4 1.9 copy.99
  898.3 5.9 all-to-all-start.5
  904.6 35.8 %all-to-all-done.5 = bf16[32,1,20,1024]{3,2,1,0:T(8,128)(2,1)} async-done(((bf16[32,1,20,1024]{3,2,1,0:T(8,128)(2,1)}), bf16[32,1,20,1024]{3,2,1,0:T(8,128)(2,1)}, u32[]{:S(2)}, u32[]{:S(2)}) %all-to-all-start.5) | async-done | bytes 1310752 | tf_op jit(solution)/shard_map/all_to_all | solution.py:173
  940.3 3.1 convert_reduce_fusion
  944.8 2.1 gather_fusion.2
  954.1 41.2 %all-reduce.17.cloned.1.call-done = f32[128,1024]{1,0:T(8,128)} async-done(((f32[128,1024]{1,0:T(8,128)}), f32[128,1024]{1,0:T(8,128)}) %all-reduce.17.cloned.1.call-update) | async-done | bytes 524304 | tf_op jit(solution)/shard_map/psum | solution.py:188
  (473 shorter events, 155.7 us)
Async XLA Ops:
  7.2 230.5 %copy-start = (bf16[1,1,1024,2,352]{2,4,3,1,0:T(8,128)(2,1)S(1)}, bf16[1,1,1024,2,352]{2,4,3,1,0:T(8,128)(2,1)}, u32[]{:S(2)}) copy-start(bf16[1,1,1024,2,352]{2,4,3,1,0:T(8,128)(2,1)} %param.26) | copy-start | bytes 4325380
  7.2 3.9 copy-start.17
  7.2 93.1 %all-gather.4.cloned.1.call-start = ((), (), s32[]{:S(2)}) async-start(), calls=%async_computation.6 | async-start | bytes 4325376 | tf_op jit(solution)/shard_map/all_gather | solution.py:120
  9.3 3.1 copy-start.38
  11.0 89.3 %copy-start.7 = (bf16[1,1024,3,256]{1,3,2,0:T(8,128)(2,1)}, bf16[1,1024,3,256]{1,3,2,0:T(8,128)(2,1)S(1)}, u32[]{:S(2)}) copy-start(bf16[1,1024,3,256]{1,3,2,0:T(8,128)(2,1)S(1)} %copy.83) | copy-start | bytes 4718596
  14.2 172.7 %all-reduce.7.cloned.1.call-start = ((), (), s32[]{:S(2)}) async-start(), calls=%async_computation.7 | async-start | bytes 1048576 | tf_op jit(solution)/shard_map/psum | solution.py:144
  16.2 84.1 %copy-start.45 = (s32[2,128]{1,0:T(2,128)}, s32[2,128]{1,0:T(2,128)S(1)}, u32[]{:S(2)}) copy-start(s32[2,128]{1,0:T(2,128)S(1)} %get-tuple-element.708) | copy-start | bytes 3076
  102.7 2.1 copy-start.21
  111.4 2.1 copy-start.21
  120.1 2.1 copy-start.21
  128.8 2.1 copy-start.21
  135.2 51.6 %copy-start.18 = (bf16[2,128,1024]{2,1,0:T(8,128)(2,1)S(1)}, bf16[2,128,1024]{2,1,0:T(8,128)(2,1)}, u32[]{:S(2)}) copy-start(bf16[2,128,1024]{2,1,0:T(8,128)(2,1)} %param.18) | copy-start | bytes 1572868
  242.3 5.8 copy-start.44
  242.3 41.9 %all-to-all-start.1 = ((bf16[32,1,20,1024]{3,2,1,0:T(8,128)(2,1)}), bf16[32,1,20,1024]{3,2,1,0:T(8,128)(2,1)S(1)}, u32[]{:S(2)}, u32[]{:S(2)}) async-start(bf16[32,1,20,1024]{3,2,1,0:T(8,128)(2,1)} %copy.87), calls=%async_computation.1 | async-start | bytes 3145728 | tf_op jit(solution)/shard_map/all_to_all | solution.py:173
  248.0 89.7 %all-reduce.9.cloned.1.call-start = ((), (), s32[]{:S(2)}) async-start(), calls=%async_computation.8 | async-start | bytes 1048576 | tf_op jit(solution)/shard_map/psum | solution.py:188
  287.2 2.2 copy-start.48
  290.7 51.6 %copy-start.8 = (bf16[1,1024,3,256]{1,3,2,0:T(8,128)(2,1)S(1)}, bf16[1,1024,3,256]{1,3,2,0:T(8,128)(2,1)}, u32[]{:S(2)}) copy-start(bf16[1,1024,3,256]{1,3,2,0:T(8,128)(2,1)} %copy-done.7) | copy-start | bytes 4718596
  290.7 51.6 %copy-start.39 = (f32[1,1,1024]{2,1,0:T(1,128)S(1)}, f32[1,1,1024]{2,1,0:T(1,128)}, u32[]{:S(2)}) copy-start(f32[1,1,1024]{2,1,0:T(1,128)} %copy-done.38) | copy-start | bytes 12292
  291.7 136.0 %all-gather.6.cloned.1.call-start = ((), (), s32[]{:S(2)}) async-start(), calls=%async_computation.9 | async-start | bytes 4325376 | tf_op jit(solution)/shard_map/all_gather | solution.py:120
  339.0 2.6 copy-start.28
  339.0 2.4 collective-permute-start
  343.9 170.4 %all-reduce.11.cloned.1.call-start = ((), (), s32[]{:S(2)}) async-start(), calls=%async_computation.10 | async-start | bytes 1048576 | tf_op jit(solution)/shard_map/psum | solution.py:144
  345.2 82.5 %copy-start.31 = (s32[16,2,128]{2,0,1:T(8,128)}, s32[16,2,128]{2,0,1:T(8,128)S(1)}, u32[]{:S(2)}) copy-start(s32[16,2,128]{2,0,1:T(8,128)S(1)} %reduce-window.24) | copy-start | bytes 49156
  430.1 2.1 copy-start.23
  462.7 51.6 %copy-start.16 = (bf16[128,1024]{1,0:T(8,128)(2,1)S(1)}, bf16[128,1024]{1,0:T(8,128)(2,1)}, u32[]{:S(2)}) copy-start(bf16[128,1024]{1,0:T(8,128)(2,1)} %copy-done.15) | copy-start | bytes 786436
  569.0 5.8 copy-start.42
  569.0 41.9 %all-to-all-start.3 = ((bf16[32,1,20,1024]{3,2,1,0:T(8,128)(2,1)}), bf16[32,1,20,1024]{3,2,1,0:T(8,128)(2,1)S(1)}, u32[]{:S(2)}, u32[]{:S(2)}) async-start(bf16[32,1,20,1024]{3,2,1,0:T(8,128)(2,1)} %copy.93), calls=%async_computation.3 | async-start | bytes 3145728 | tf_op jit(solution)/shard_map/all_to_all | solution.py:173
  574.7 89.8 %all-reduce.13.cloned.1.call-start = ((), (), s32[]{:S(2)}) async-start(), calls=%async_computation.11 | async-start | bytes 1048576 | tf_op jit(solution)/shard_map/psum | solution.py:188
  613.8 2.2 copy-start.49
  616.0 48.5 %copy-start.29 = (bf16[128,1024]{1,0:T(8,128)(2,1)S(1)}, bf16[128,1024]{1,0:T(8,128)(2,1)}, u32[]{:S(2)}) copy-start(bf16[128,1024]{1,0:T(8,128)(2,1)} %copy-done.28) | copy-start | bytes 786436
  618.4 51.6 %copy-start.9 = (bf16[1,1024,3,256]{1,3,2,0:T(8,128)(2,1)S(1)}, bf16[1,1024,3,256]{1,3,2,0:T(8,128)(2,1)}, u32[]{:S(2)}) copy-start(bf16[1,1024,3,256]{1,3,2,0:T(8,128)(2,1)} %copy-done.7) | copy-start | bytes 4718596
  618.4 51.6 %copy-start.40 = (f32[1,1,1024]{2,1,0:T(1,128)S(1)}, f32[1,1,1024]{2,1,0:T(1,128)}, u32[]{:S(2)}) copy-start(f32[1,1,1024]{2,1,0:T(1,128)} %copy-done.38) | copy-start | bytes 12292
  618.4 136.9 %all-gather.8.cloned.1.call-start = ((), (), s32[]{:S(2)}) async-start(), calls=%async_computation.12 | async-start | bytes 4325376 | tf_op jit(solution)/shard_map/all_gather | solution.py:120
  664.5 4.6 copy-start.19
  666.6 2.6 copy-start.25
  666.6 2.4 collective-permute-start.1
  671.5 170.2 %all-reduce.15.cloned.1.call-start = ((), (), s32[]{:S(2)}) async-start(), calls=%async_computation.13 | async-start | bytes 1048576 | tf_op jit(solution)/shard_map/psum | solution.py:144
  790.0 51.6 %copy-start.14 = (bf16[128,1024]{1,0:T(8,128)(2,1)S(1)}, bf16[128,1024]{1,0:T(8,128)(2,1)}, u32[]{:S(2)}) copy-start(bf16[128,1024]{1,0:T(8,128)(2,1)} %copy-done.13) | copy-start | bytes 786436
  898.3 5.9 copy-start.41
  898.3 5.9 copy-start.43
  898.3 6.0 copy-start.30
  898.3 6.2 copy-start.46
  898.3 42.0 %all-to-all-start.5 = ((bf16[32,1,20,1024]{3,2,1,0:T(8,128)(2,1)}), bf16[32,1,20,1024]{3,2,1,0:T(8,128)(2,1)}, u32[]{:S(2)}, u32[]{:S(2)}) async-start(bf16[32,1,20,1024]{3,2,1,0:T(8,128)(2,1)} %copy.99), calls=%async_computation.5 | async-start | bytes 3145728 | tf_op jit(solution)/shard_map/all_to_all | solution.py:173
  904.2 91.1 %all-reduce.17.cloned.1.call-start = ((), (), s32[]{:S(2)}) async-start(), calls=%async_computation.14 | async-start | bytes 1048576 | tf_op jit(solution)/shard_map/psum | solution.py:188
  946.9 2.3 copy-start.47
  948.3 46.9 %copy-start.20 = (f32[128,1024]{1,0:T(8,128)S(1)}, f32[128,1024]{1,0:T(8,128)}, u32[]{:S(2)}) copy-start(f32[128,1024]{1,0:T(8,128)} %all-reduce.15.cloned.1.call-done) | copy-start | bytes 1572868
  948.3 46.9 %copy-start.26 = (bf16[128,1024]{1,0:T(8,128)(2,1)S(1)}, bf16[128,1024]{1,0:T(8,128)(2,1)}, u32[]{:S(2)}) copy-start(bf16[128,1024]{1,0:T(8,128)(2,1)} %copy-done.25) | copy-start | bytes 786436
  949.2 47.2 %copy-start.27 = (bf16[1,128,1024]{2,1,0:T(8,128)(2,1)S(1)}, bf16[1,128,1024]{2,1,0:T(8,128)(2,1)}, u32[]{:S(2)}) copy-start(bf16[1,128,1024]{2,1,0:T(8,128)(2,1)} %get-tuple-element.669) | copy-start | bytes 786436
  (73 other events, 111.8 us)
Sparse Core Ops, SparseCore 0:
  14.3 85.9 all-gather.3
  138.5 48.3 all-reduce.6
  291.8 45.8 all-reduce.8
  344.0 83.6 all-gather.5
  465.9 48.3 all-reduce.10
  618.5 45.9 all-reduce.12
  671.6 83.6 all-gather.7
  793.3 48.3 all-reduce.14
  949.4 45.8 all-reduce.16
where the time goes:
time: 1010 us; the launch traced here: 1000 us
  waiting for transfers between devices  619 us (61%)
  blocking collectives  141 us (14%)
  other arithmetic  82.9 us (8%)
  local copies, waits for them, and re-layouts  77.7 us (8%)
  matrix products  45.3 us (4%)
  starting transfers between devices  20.6 us (2%)
  between operations  16.4 us (2%)
    all_gather x3, waiting for transfers between devices, per_device(): piece = lax.all_gather(keys_vals, 'tok', axis=0, tiled=True)  242 us
    all_to_all x3, blocking collectives, per_device(): lax.all_to_all(copies, 'tok', split_axis=0, concat_axis=0, tiled=True)  141 us
    psum x3, waiting for transfers between devices, per_device(): mid = resid + lax.psum(attn_part, 'rep')  139 us
    psum x3, waiting for transfers between devices, per_device(): expert_total = lax.psum(expert_local, 'rep')  133 us
    all_to_all x3, waiting for transfers between devices, per_device(): lax.all_to_all(jnp.einsum('secf,efd->secd', hidden, w_down, preferred_ele...  102 us
    slice x12, local copies, waits for them, and re-layouts, attend(): keys_vals[:, 1].reshape(rows_key, heads_here, head_size).astype(jnp.float32)  25.2 us
  transfers between devices with their start and end apart: 14, of which 14 were waited for; matrix products, arithmetic and copies ran while one was open for 3% of the time, Pallas kernels for 0%

commit v1 on v0

--- a/solution.py
+++ b/solution.py
@@ -185,7 +185,11 @@
         summed = summed.reshape(experts_all * CAP, width)
         gathered = jnp.take(summed, flat_slot, axis=0).reshape(TOP, tok_rows, width)
         expert_local = jnp.sum(gate_vals.T[:, :, None] * gathered, axis=0)
-        expert_total = lax.psum(expert_local, "rep")
+        expert_total = expert_local
+        for hop in (1, 2):
+            expert_total = expert_total + lax.ppermute(
+                expert_total, "rep", [(dev, dev ^ hop) for dev in range(4)]
+            )
         layer_result = (mid + expert_total).astype(jnp.bfloat16)
         for slot_micro in range(micro_count):
             if slot_micro == round_index or slot_micro == round_index - 1:

time: 1010 us -> 946 us (0.937)
  waiting for transfers between devices: 619 us -> 536 us
  starting transfers between devices: 20.6 us -> 36.6 us
    psum x3 -> x0, waiting for transfers between devices: 133 us -> none  [per_device(): expert_total = lax.psum(expert_local, 'rep')]
    ppermute x0 -> x6, waiting for transfers between devices: none -> 56.6 us  [per_device(): lax.ppermute(expert_total, 'rep', [(dev, dev ^ hop) for dev in range(4)])]
    ppermute x0 -> x6, starting transfers between devices: none -> 16.3 us  [per_device(): lax.ppermute(expert_total, 'rep', [(dev, dev ^ hop) for dev in range(4)])]
  transfers between devices with their start and end apart: 14 -> 17, of which waited for: 14 -> 17; matrix products, arithmetic and copies ran while one was open for 3% -> 3% of each run, Pallas kernels for 0% -> 0%
where the time goes in v1:
time: 946 us; the launch traced here: 935 us
  waiting for transfers between devices  536 us (57%)
  blocking collectives  141 us (15%)
  other arithmetic  79.2 us (8%)
  local copies, waits for them, and re-layouts  77.8 us (8%)
  matrix products  45.3 us (5%)
  starting transfers between devices  36.6 us (4%)
  between operations  17.2 us (2%)
    all_gather x3, waiting for transfers between devices, per_device(): piece = lax.all_gather(keys_vals, 'tok', axis=0, tiled=True)  236 us
    all_to_all x3, blocking collectives, per_device(): lax.all_to_all(copies, 'tok', split_axis=0, concat_axis=0, tiled=True)  141 us
    psum x3, waiting for transfers between devices, per_device(): mid = resid + lax.psum(attn_part, 'rep')  139 us
    all_to_all x3, waiting for transfers between devices, per_device(): lax.all_to_all(jnp.einsum('secf,efd->secd', hidden, w_down, preferred_ele...  102 us
    ppermute x6, waiting for transfers between devices, per_device(): lax.ppermute(expert_total, 'rep', [(dev, dev ^ hop) for dev in range(4)])  56.6 us
    slice x12, local copies, waits for them, and re-layouts, attend(): keys_vals[:, 1].reshape(rows_key, heads_here, head_size).astype(jnp.float32)  25.2 us
    and x12, other arithmetic, attend(): (seg_query[:, None] == seg_key[None, :]) & (pos_query[:, None] >= pos_key...  19.7 us
  transfers between devices with their start and end apart: 17, of which 17 were waited for; matrix products, arithmetic and copies ran while one was open for 3% of the time, Pallas kernels for 0%

profile of v1, /device:TPU:8, one launch (start us, length us, event | category | flops | bytes accessed | tf_op | source)
XLA Modules:
  0.0 934.6 jit_solution(10413187388867656130)
XLA Ops:
  20.4 79.9 %all-gather.4.cloned.1.call-done = bf16[4096,2,256]{0,2,1:T(8,128)(2,1)} async-done(((bf16[128,2,256]{0,2,1:T(8,128)(2,1)}), bf16[4096,2,256]{0,2,1:T(8,128)(2,1)}) %all-gather.4.cloned.1.call-update) | async-done | bytes 4194320 | tf_op jit(solution)/shard_map/all_gather | solution.py:120
  100.3 34.9 %while.54 = (s32[]{:T(128)}, f32[4,128]{1,0:T(4,128)S(1)}, f32[4,128]{1,0:T(4,128)S(1)}, f32[4,128,64]{1,2,0:T(8,128)}, s32[128]{0:T(128)}, /*index=5*/s32[4096]...) while((s32[]{:T(128)}, f32[4,128]{1,0:T(4,128)S(1)}, ...), condition=%wide.region_4.5_spmd.clone, body=%wide.region_1.4_spmd.clone.sunk | while | flops 476548736 | bytes 14800775 | solution.py:134
  102.7 2.1 constant_dynamic-slice_fusion.18
  111.4 2.1 constant_dynamic-slice_fusion.18
  120.1 2.1 constant_dynamic-slice_fusion.18
  128.8 2.1 constant_dynamic-slice_fusion.18
  136.2 2.1 fusion.102
  140.8 46.1 %all-reduce.4.cloned.1.call-done = f32[128,1024]{1,0:T(8,128)} async-done(((f32[128,1024]{1,0:T(8,128)}), f32[128,1024]{1,0:T(8,128)}) %all-reduce.4.cloned.1.call-update) | async-done | bytes 524304 | tf_op jit(solution)/shard_map/psum | solution.py:144
  190.6 47.1 %all_to_all.30 = bf16[32,1,20,1024]{3,2,1,0:T(8,128)(2,1)S(1)} all-to-all(bf16[32,1,20,1024]{3,2,1,0:T(8,128)(2,1)S(1)} %bitcast.386), channel_id=1, replica_groups=mesh['section'=2,'tok'=32,'rep'=4] {'tok'}, dimensions={0} | all-to-all | bytes 2621440 | tf_op jit(solution)/shard_map/all_to_all | solution.py:168
  240.4 1.9 copy.87
  242.3 5.7 all-to-all-start.1
  251.2 33.0 %all-to-all-done.1 = bf16[32,1,20,1024]{3,2,1,0:T(8,128)(2,1)S(1)} async-done(((bf16[32,1,20,1024]{3,2,1,0:T(8,128)(2,1)}), bf16[32,1,20,1024]{3,2,1,0:T(8,128)(2,1)S(1)}, u32[]{:S(2)}, u32[]{:S(2)}) %all-to-all-start.1) | async-done | bytes 1310752 | tf_op jit(solution)/shard_map/all_to_all | solution.py:173
  287.2 2.2 gather_fusion
  292.5 10.6 %collective-permute-done = f32[128,1024]{1,0:T(8,128)S(1)} collective-permute-done((f32[128,1024]{1,0:T(8,128)S(1)}, f32[128,1024]{1,0:T(8,128)S(1)}, u32[]{:S(2)}, u32[]{:S(2)}) %collective-permute-start) | collective-permute-done | bytes 524320 | tf_op jit(solution)/shard_map/ppermute | solution.py:190
  303.2 3.9 collective-permute-start.1
  307.1 9.8 %collective-permute-done.1 = f32[128,1024]{1,0:T(8,128)S(1)} collective-permute-done((f32[128,1024]{1,0:T(8,128)S(1)}, f32[128,1024]{1,0:T(8,128)S(1)}, u32[]{:S(2)}, u32[]{:S(2)}) %collective-permute-start.1) | collective-permute-done | bytes 524320 | tf_op jit(solution)/shard_map/ppermute | solution.py:190
  325.4 76.7 %all-gather.6.cloned.1.call-done = bf16[4096,2,256]{0,2,1:T(8,128)(2,1)} async-done(((bf16[128,2,256]{0,2,1:T(8,128)(2,1)}), bf16[4096,2,256]{0,2,1:T(8,128)(2,1)}) %all-gather.6.cloned.1.call-update) | async-done | bytes 4194320 | tf_op jit(solution)/shard_map/all_gather | solution.py:120
  402.1 35.0 %while.55 = (s32[]{:T(128)}, f32[4,128]{1,0:T(4,128)S(1)}, f32[4,128]{1,0:T(4,128)S(1)}, f32[4,128,64]{1,2,0:T(8,128)}, s32[128]{0:T(128)}, /*index=5*/s32[4096]...) while((s32[]{:T(128)}, f32[4,128]{1,0:T(4,128)S(1)}, ...), condition=%wide.region_20.22_spmd.clone, body=%wide.region_17.21_spmd.clone.sunk | while | flops 476548736 | bytes 14800775 | solution.py:134
  404.5 2.1 constant_dynamic-slice_fusion.19
  413.2 2.1 constant_dynamic-slice_fusion.19
  422.0 2.1 constant_dynamic-slice_fusion.19
  430.7 2.1 constant_dynamic-slice_fusion.19
  438.0 2.1 fusion.100
  443.2 45.5 %all-reduce.6.cloned.1.call-done = f32[128,1024]{1,0:T(8,128)} async-done(((f32[128,1024]{1,0:T(8,128)}), f32[128,1024]{1,0:T(8,128)}) %all-reduce.6.cloned.1.call-update) | async-done | bytes 524304 | tf_op jit(solution)/shard_map/psum | solution.py:144
  491.7 47.1 %all_to_all.31 = bf16[32,1,20,1024]{3,2,1,0:T(8,128)(2,1)S(1)} all-to-all(bf16[32,1,20,1024]{3,2,1,0:T(8,128)(2,1)S(1)} %bitcast.387), channel_id=1, replica_groups=mesh['section'=2,'tok'=32,'rep'=4] {'tok'}, dimensions={0} | all-to-all | bytes 2621440 | tf_op jit(solution)/shard_map/all_to_all | solution.py:168
  543.4 5.7 all-to-all-start.3
  552.0 33.2 %all-to-all-done.3 = bf16[32,1,20,1024]{3,2,1,0:T(8,128)(2,1)S(1)} async-done(((bf16[32,1,20,1024]{3,2,1,0:T(8,128)(2,1)}), bf16[32,1,20,1024]{3,2,1,0:T(8,128)(2,1)S(1)}, u32[]{:S(2)}, u32[]{:S(2)}) %all-to-all-start.3) | async-done | bytes 1310752 | tf_op jit(solution)/shard_map/all_to_all | solution.py:173
  588.2 2.2 gather_fusion.1
  593.6 10.6 %collective-permute-done.3 = f32[128,1024]{1,0:T(8,128)S(1)} collective-permute-done((f32[128,1024]{1,0:T(8,128)S(1)}, f32[128,1024]{1,0:T(8,128)S(1)}, u32[]{:S(2)}, u32[]{:S(2)}) %collective-permute-start.3) | collective-permute-done | bytes 524320 | tf_op jit(solution)/shard_map/ppermute | solution.py:190
  605.1 3.8 collective-permute-start.4
  608.9 10.1 %collective-permute-done.4 = f32[128,1024]{1,0:T(8,128)} collective-permute-done((f32[128,1024]{1,0:T(8,128)}, f32[128,1024]{1,0:T(8,128)}, u32[]{:S(2)}, u32[]{:S(2)}) %collective-permute-start.4) | collective-permute-done | bytes 524320 | tf_op jit(solution)/shard_map/ppermute | solution.py:190
  619.0 2.3 select_bitcast_fusion
  626.8 79.4 %all-gather.8.cloned.1.call-done = bf16[4096,2,256]{0,2,1:T(8,128)(2,1)} async-done(((bf16[128,2,256]{0,2,1:T(8,128)(2,1)}), bf16[4096,2,256]{0,2,1:T(8,128)(2,1)}) %all-gather.8.cloned.1.call-update) | async-done | bytes 4194320 | tf_op jit(solution)/shard_map/all_gather | solution.py:120
  706.2 34.7 %while.56 = (s32[]{:T(128)}, f32[4,128]{1,0:T(4,128)S(1)}, f32[4,128]{1,0:T(4,128)S(1)}, f32[4,128,64]{1,2,0:T(8,128)}, s32[128]{0:T(128)}, /*index=5*/s32[4096]...) while((s32[]{:T(128)}, f32[4,128]{1,0:T(4,128)S(1)}, ...), condition=%wide.region_36.38_spmd.clone, body=%wide.region_33.37_spmd.clone.sunk | while | flops 476548736 | bytes 14800775 | solution.py:134
  708.5 2.1 constant_dynamic-slice_fusion.20
  717.2 2.1 constant_dynamic-slice_fusion.20
  725.9 2.1 constant_dynamic-slice_fusion.20
  734.6 2.1 constant_dynamic-slice_fusion.20
  741.9 2.1 fusion.98
  744.8 47.8 %all-reduce.8.cloned.1.call-done = f32[128,1024]{1,0:T(8,128)} async-done(((f32[128,1024]{1,0:T(8,128)}), f32[128,1024]{1,0:T(8,128)}) %all-reduce.8.cloned.1.call-update) | async-done | bytes 524304 | tf_op jit(solution)/shard_map/psum | solution.py:144
  797.5 47.1 %all_to_all.32 = bf16[32,1,20,1024]{3,2,1,0:T(8,128)(2,1)S(1)} all-to-all(bf16[32,1,20,1024]{3,2,1,0:T(8,128)(2,1)S(1)} %bitcast.388), channel_id=1, replica_groups=mesh['section'=2,'tok'=32,'rep'=4] {'tok'}, dimensions={0} | all-to-all | bytes 2621440 | tf_op jit(solution)/shard_map/all_to_all | solution.py:168
  849.2 5.9 all-to-all-start.5
  855.4 35.8 %all-to-all-done.5 = bf16[32,1,20,1024]{3,2,1,0:T(8,128)(2,1)} async-done(((bf16[32,1,20,1024]{3,2,1,0:T(8,128)(2,1)}), bf16[32,1,20,1024]{3,2,1,0:T(8,128)(2,1)}, u32[]{:S(2)}, u32[]{:S(2)}) %all-to-all-start.5) | async-done | bytes 1310752 | tf_op jit(solution)/shard_map/all_to_all | solution.py:173
  891.2 3.1 convert_reduce_fusion
  895.7 2.1 gather_fusion.2
  901.0 10.6 %collective-permute-done.6 = f32[128,1024]{1,0:T(8,128)S(1)} collective-permute-done((f32[128,1024]{1,0:T(8,128)S(1)}, f32[128,1024]{1,0:T(8,128)S(1)}, u32[]{:S(2)}, u32[]{:S(2)}) %collective-permute-start.6) | collective-permute-done | bytes 524320 | tf_op jit(solution)/shard_map/ppermute | solution.py:190
  911.7 3.7 collective-permute-start.7
  920.3 5.0 collective-permute-done.7
  (485 shorter events, 167.4 us)
Async XLA Ops:
  7.2 230.5 %copy-start = (bf16[1,1,1024,2,352]{2,4,3,1,0:T(8,128)(2,1)S(1)}, bf16[1,1,1024,2,352]{2,4,3,1,0:T(8,128)(2,1)}, u32[]{:S(2)}) copy-start(bf16[1,1,1024,2,352]{2,4,3,1,0:T(8,128)(2,1)} %param.26) | copy-start | bytes 4325380
  7.2 3.9 copy-start.17
  7.2 93.1 %all-gather.4.cloned.1.call-start = ((), (), s32[]{:S(2)}) async-start(), calls=%async_computation.6 | async-start | bytes 4325376 | tf_op jit(solution)/shard_map/all_gather | solution.py:120
  9.3 3.1 copy-start.39
  11.0 89.3 %copy-start.7 = (bf16[1,1024,3,256]{1,3,2,0:T(8,128)(2,1)}, bf16[1,1024,3,256]{1,3,2,0:T(8,128)(2,1)S(1)}, u32[]{:S(2)}) copy-start(bf16[1,1024,3,256]{1,3,2,0:T(8,128)(2,1)S(1)} %copy.83) | copy-start | bytes 4718596
  14.2 172.7 %all-reduce.4.cloned.1.call-start = ((), (), s32[]{:S(2)}) async-start(), calls=%async_computation.7 | async-start | bytes 1048576 | tf_op jit(solution)/shard_map/psum | solution.py:144
  16.2 84.1 %copy-start.48 = (s32[2,128]{1,0:T(2,128)}, s32[2,128]{1,0:T(2,128)S(1)}, u32[]{:S(2)}) copy-start(s32[2,128]{1,0:T(2,128)S(1)} %get-tuple-element.708) | copy-start | bytes 3076
  135.2 51.6 %copy-start.18 = (bf16[2,128,1024]{2,1,0:T(8,128)(2,1)S(1)}, bf16[2,128,1024]{2,1,0:T(8,128)(2,1)}, u32[]{:S(2)}) copy-start(bf16[2,128,1024]{2,1,0:T(8,128)(2,1)} %param.18) | copy-start | bytes 1572868
  242.3 5.8 copy-start.47
  242.3 41.9 %all-to-all-start.1 = ((bf16[32,1,20,1024]{3,2,1,0:T(8,128)(2,1)}), bf16[32,1,20,1024]{3,2,1,0:T(8,128)(2,1)S(1)}, u32[]{:S(2)}, u32[]{:S(2)}) async-start(bf16[32,1,20,1024]{3,2,1,0:T(8,128)(2,1)} %copy.87), calls=%async_computation.1 | async-start | bytes 3145728 | tf_op jit(solution)/shard_map/all_to_all | solution.py:173
  248.0 154.1 %all-gather.6.cloned.1.call-start = ((), (), s32[]{:S(2)}) async-start(), calls=%async_computation.8 | async-start | bytes 4325376 | tf_op jit(solution)/shard_map/all_gather | solution.py:120
  287.2 2.2 copy-start.51
  290.7 26.1 %copy-start.20 = (f32[128,1024]{1,0:T(8,128)S(1)}, f32[128,1024]{1,0:T(8,128)}, u32[]{:S(2)}) copy-start(f32[128,1024]{1,0:T(8,128)} %all-reduce.4.cloned.1.call-done) | copy-start | bytes 1572868
  290.9 29.6 %copy-start.8 = (bf16[1,1024,3,256]{1,3,2,0:T(8,128)(2,1)S(1)}, bf16[1,1024,3,256]{1,3,2,0:T(8,128)(2,1)}, u32[]{:S(2)}) copy-start(bf16[1,1024,3,256]{1,3,2,0:T(8,128)(2,1)} %copy-done.7) | copy-start | bytes 4718596
  290.9 29.6 %copy-start.40 = (f32[1,1,1024]{2,1,0:T(1,128)S(1)}, f32[1,1,1024]{2,1,0:T(1,128)}, u32[]{:S(2)}) copy-start(f32[1,1,1024]{2,1,0:T(1,128)} %copy-done.39) | copy-start | bytes 12292
  290.9 12.3 %collective-permute-start = (f32[128,1024]{1,0:T(8,128)S(1)}, f32[128,1024]{1,0:T(8,128)S(1)}, u32[]{:S(2)}, u32[]{:S(2)}) collective-permute-start(f32[128,1024]{1,0:T(8,128)S(1)} %multiply_reduce_fusion.2), channel_id=1, source_target_pairs={{0,1},{1,0},{2,3},{3,2},{4,5},{5,4},{6,7},{7,6},{8,9},{9,8},{10,11... | collective-permute-start | bytes 1572872 | tf_op jit(solution)/shard_map/ppermute | solution.py:190
  303.2 13.6 %collective-permute-start.1 = (f32[128,1024]{1,0:T(8,128)S(1)}, f32[128,1024]{1,0:T(8,128)S(1)}, u32[]{:S(2)}, u32[]{:S(2)}) collective-permute-start(f32[128,1024]{1,0:T(8,128)S(1)} %add.387), channel_id=1, source_target_pairs={{0,2},{1,3},{2,0},{3,1},{4,6},{5,7},{6,4},{7,5},{8,10},{9,11},{10,... | collective-permute-start | bytes 1572872 | tf_op jit(solution)/shard_map/ppermute | solution.py:190
  317.0 2.8 copy-start.28
  317.0 5.1 copy-start.45
  317.0 6.5 copy-start.43
  317.0 2.6 collective-permute-start.2
  322.0 166.7 %all-reduce.6.cloned.1.call-start = ((), (), s32[]{:S(2)}) async-start(), calls=%async_computation.9 | async-start | bytes 1048576 | tf_op jit(solution)/shard_map/psum | solution.py:144
  322.7 79.4 %copy-start.32 = (s32[16,2,128]{2,0,1:T(8,128)}, s32[16,2,128]{2,0,1:T(8,128)S(1)}, u32[]{:S(2)}) copy-start(s32[16,2,128]{2,0,1:T(8,128)S(1)} %reduce-window.24) | copy-start | bytes 49156
  437.1 51.6 %copy-start.16 = (bf16[128,1024]{1,0:T(8,128)(2,1)S(1)}, bf16[128,1024]{1,0:T(8,128)(2,1)}, u32[]{:S(2)}) copy-start(bf16[128,1024]{1,0:T(8,128)(2,1)} %copy-done.15) | copy-start | bytes 786436
  543.4 5.8 copy-start.44
  543.4 41.9 %all-to-all-start.3 = ((bf16[32,1,20,1024]{3,2,1,0:T(8,128)(2,1)}), bf16[32,1,20,1024]{3,2,1,0:T(8,128)(2,1)S(1)}, u32[]{:S(2)}, u32[]{:S(2)}) async-start(bf16[32,1,20,1024]{3,2,1,0:T(8,128)(2,1)} %copy.93), calls=%async_computation.3 | async-start | bytes 3145728 | tf_op jit(solution)/shard_map/all_to_all | solution.py:173
  549.1 157.1 %all-gather.8.cloned.1.call-start = ((), (), s32[]{:S(2)}) async-start(), calls=%async_computation.10 | async-start | bytes 4325376 | tf_op jit(solution)/shard_map/all_gather | solution.py:120
  588.2 2.2 copy-start.52
  591.8 27.2 %copy-start.29 = (bf16[128,1024]{1,0:T(8,128)(2,1)S(1)}, bf16[128,1024]{1,0:T(8,128)(2,1)}, u32[]{:S(2)}) copy-start(bf16[128,1024]{1,0:T(8,128)(2,1)} %copy-done.28) | copy-start | bytes 786436
  591.9 12.3 %collective-permute-start.3 = (f32[128,1024]{1,0:T(8,128)S(1)}, f32[128,1024]{1,0:T(8,128)S(1)}, u32[]{:S(2)}, u32[]{:S(2)}) collective-permute-start(f32[128,1024]{1,0:T(8,128)S(1)} %multiply_reduce_fusion.1), channel_id=1, source_target_pairs={{0,1},{1,0},{2,3},{3,2},{4,5},{5,4},{6,7},{7,6},{8,9},{9,8},{10,11... | collective-permute-start | bytes 1572872 | tf_op jit(solution)/shard_map/ppermute | solution.py:190
  605.1 19.5 %copy-start.9 = (bf16[1,1024,3,256]{1,3,2,0:T(8,128)(2,1)S(1)}, bf16[1,1024,3,256]{1,3,2,0:T(8,128)(2,1)}, u32[]{:S(2)}) copy-start(bf16[1,1024,3,256]{1,3,2,0:T(8,128)(2,1)} %copy-done.7) | copy-start | bytes 4718596
  605.1 19.5 %copy-start.41 = (f32[1,1,1024]{2,1,0:T(1,128)S(1)}, f32[1,1,1024]{2,1,0:T(1,128)}, u32[]{:S(2)}) copy-start(f32[1,1,1024]{2,1,0:T(1,128)} %copy-done.39) | copy-start | bytes 12292
  605.1 13.9 %collective-permute-start.4 = (f32[128,1024]{1,0:T(8,128)}, f32[128,1024]{1,0:T(8,128)}, u32[]{:S(2)}, u32[]{:S(2)}) collective-permute-start(f32[128,1024]{1,0:T(8,128)} %add.397), channel_id=1, source_target_pairs={{0,2},{1,3},{2,0},{3,1},{4,6},{5,7},{6,4},{7,5},{8,10},{9,11},{10,... | collective-permute-start | bytes 1572872 | tf_op jit(solution)/shard_map/ppermute | solution.py:190
  608.9 14.8 %copy-start.19 = (bf16[2,128,1024]{2,1,0:T(8,128)(2,1)S(1)}, bf16[2,128,1024]{2,1,0:T(8,128)(2,1)}, u32[]{:S(2)}) copy-start(bf16[2,128,1024]{2,1,0:T(8,128)(2,1)} %param.18) | copy-start | bytes 1572868
  621.2 2.4 collective-permute-start.5
  626.1 166.5 %all-reduce.8.cloned.1.call-start = ((), (), s32[]{:S(2)}) async-start(), calls=%async_computation.11 | async-start | bytes 1048576 | tf_op jit(solution)/shard_map/psum | solution.py:144
  740.9 51.6 %copy-start.14 = (bf16[128,1024]{1,0:T(8,128)(2,1)S(1)}, bf16[128,1024]{1,0:T(8,128)(2,1)}, u32[]{:S(2)}) copy-start(bf16[128,1024]{1,0:T(8,128)(2,1)} %copy-done.13) | copy-start | bytes 786436
  849.2 5.9 copy-start.42
  849.2 5.9 copy-start.46
  849.2 5.9 copy-start.31
  849.2 6.1 copy-start.49
  849.2 42.0 %all-to-all-start.5 = ((bf16[32,1,20,1024]{3,2,1,0:T(8,128)(2,1)}), bf16[32,1,20,1024]{3,2,1,0:T(8,128)(2,1)}, u32[]{:S(2)}, u32[]{:S(2)}) async-start(bf16[32,1,20,1024]{3,2,1,0:T(8,128)(2,1)} %copy.99), calls=%async_computation.5 | async-start | bytes 3145728 | tf_op jit(solution)/shard_map/all_to_all | solution.py:173
  899.2 16.2 %copy-start.50 = (s32[2,32]{1,0:T(2,128)S(1)}, s32[2,32]{1,0:T(2,128)}, u32[]{:S(2)}) copy-start(s32[2,32]{1,0:T(2,128)} %param.21) | copy-start | bytes 772
  899.2 26.1 %copy-start.21 = (f32[128,1024]{1,0:T(8,128)S(1)}, f32[128,1024]{1,0:T(8,128)}, u32[]{:S(2)}) copy-start(f32[128,1024]{1,0:T(8,128)} %all-reduce.8.cloned.1.call-done) | copy-start | bytes 1572868
  899.2 26.1 %copy-start.27 = (bf16[128,1024]{1,0:T(8,128)(2,1)S(1)}, bf16[128,1024]{1,0:T(8,128)(2,1)}, u32[]{:S(2)}) copy-start(bf16[128,1024]{1,0:T(8,128)(2,1)} %copy-done.26) | copy-start | bytes 786436
  899.3 12.2 %collective-permute-start.6 = (f32[128,1024]{1,0:T(8,128)S(1)}, f32[128,1024]{1,0:T(8,128)S(1)}, u32[]{:S(2)}, u32[]{:S(2)}) collective-permute-start(f32[128,1024]{1,0:T(8,128)S(1)} %multiply_reduce_fusion), channel_id=1, source_target_pairs={{0,1},{1,0},{2,3},{3,2},{4,5},{5,4},{6,7},{7,6},{8,9},{9,8},{10,11... | collective-permute-start | bytes 1572872 | tf_op jit(solution)/shard_map/ppermute | solution.py:190
  911.7 14.8 %copy-start.30 = (bf16[1,128,1024]{2,1,0:T(8,128)(2,1)S(1)}, bf16[1,128,1024]{2,1,0:T(8,128)(2,1)}, u32[]{:S(2)}) copy-start(bf16[1,128,1024]{2,1,0:T(8,128)(2,1)} %get-tuple-element.669) | copy-start | bytes 786436
  911.7 13.6 %collective-permute-start.7 = (f32[128,1024]{1,0:T(8,128)S(1)}, f32[128,1024]{1,0:T(8,128)}, u32[]{:S(2)}, u32[]{:S(2)}) collective-permute-start(f32[128,1024]{1,0:T(8,128)S(1)} %add.407), channel_id=1, source_target_pairs={{0,2},{1,3},{2,0},{3,1},{4,6},{5,7},{6,4},{7,5},{8,10},{9,11},{10,... | collective-permute-start | bytes 1572872 | tf_op jit(solution)/shard_map/ppermute | solution.py:190
  (79 other events, 123.7 us)
Sparse Core Ops, SparseCore 0:
  14.3 85.9 all-gather.3
  138.5 48.3 all-reduce.3
  322.2 79.9 all-gather.5
  440.3 48.3 all-reduce.5
  626.2 79.9 all-gather.7
  744.2 48.3 all-reduce.7
